TPU v7x, 32 devices: a whole 2x2x4 slice. The times are simulated.
32 devices in a mesh: case: 2 (over y), tm: 4 (over z), bundle: 2 (over x), sub: 2 (over core).
Axes of the slice: x: 2, y: 2, z: 4, core: 2. Of those that a mesh axis runs over, the one named last changes fastest.
Arguments:
- cotangent: bfloat16 [16384, 512], P(('case', 'tm'), 'bundle'), parts along dimension 0, may hold values from -28 to 28
- inputs: bfloat16 [16384, 512], P(('case', 'tm'), 'bundle'), parts along dimension 0, may hold values from -6 to 6
- impulse: bfloat16 [8, 128, 4096], P('bundle', 'sub'), may hold values from -0.0625 to 0.0625
- terminal: int32 [8, 64], P('bundle'), may hold values from 0 to 63, each once within a row
- fault_step: int32 [2], P('case'), parts along dimension 0, may hold values from 0 to 4095
Outputs:
- voltage_grad: bfloat16 [16384, 512], P(('case', 'tm', 'sub'), 'bundle'), parts along dimension 0
- impulse_grad: float32 [16, 128, 4096], P(('case', 'bundle'), 'sub', 'tm'), parts along dimension 0
There are 2 independent parts, one for each index of `case`. A program takes and returns all parts, laid end to end along the dimension named above; an argument that names none is the same for every part. Nothing has to cross between parts.
Inputs may be any that keep to these rules, and one draw needn't show every extreme that they name: Each row of terminal orders the 64 terminals of a bundle, each once.
All inputs are finite; a program needn't handle non-finite values.
Results may differ from a plain program's by a relative error of at most 0.001.
Values may be sent and summed in bfloat16 or wider, within the bound.
No kernel may reach another device: no remote copies, remote signals or barrier semaphores. Data moves between devices by JAX's collectives and lax.ppermute only.
A program may use at most 320 MiB of HBM per device.

v0:
```python
import math
import jax
import jax.numpy as jnp
from jax import lax
from jax.sharding import PartitionSpec as P

CB = 64
NB = 8
L = 128
norm_ratio = 0.5
tile_rows = 8


def passed_along(block, axis, distance):
    devices = range(lax.axis_size(axis))
    route = [(i - distance, i) for i in devices if i - distance in devices]
    return lax.ppermute(block, axis, route)


def tiles_of(source, start, block_rows, lag_count):
    bundles = source.shape[0]
    width = source.shape[2]
    window = lax.dynamic_slice_in_dim(source, start, block_rows + lag_count, 1)
    tiled = window.reshape(bundles, (block_rows + lag_count) // tile_rows, tile_rows, width)
    tile_count = block_rows // tile_rows
    spans = [tiled[:, first : first + tile_count] for first in range(lag_count // tile_rows + 1)]
    wide = jnp.concatenate(spans, axis=2)
    return wide.reshape(bundles, tile_count, (lag_count + tile_rows) * width)


def local(cotangent, inputs, impulse, terminal, fault_step):
    seg_rows = cotangent.shape[0]
    local_bundles = terminal.shape[0]
    bundle_width = terminal.shape[1]
    lag_count = impulse.shape[1]
    all_lags = lag_count * lax.axis_size("sub")
    lag_first = lax.axis_index("sub") * lag_count
    columns = jnp.arange(bundle_width, dtype=jnp.int32)
    onehot = (terminal[:, :, None] == columns[None, None, :]).astype(jnp.bfloat16)
    grad_in = cotangent.reshape(seg_rows, local_bundles, bundle_width)
    reordered = jnp.einsum(
        "tbi,bir->tbr", grad_in, onehot, preferred_element_type=jnp.float32
    ).astype(jnp.bfloat16)
    seg_start = lax.axis_index("tm") * seg_rows
    steps_here = seg_start + jnp.arange(seg_rows, dtype=jnp.int32)
    live_rows = steps_here >= fault_step[0]
    masked = jnp.where(
        live_rows[:, None, None],
        inputs.reshape(seg_rows, local_bundles, bundle_width),
        jnp.zeros((), jnp.bfloat16),
    )
    ahead_rows = passed_along(reordered[:all_lags], "tm", -1)
    extended = jnp.concatenate([reordered, ahead_rows], axis=0)
    ext_lanes = jnp.transpose(extended, (1, 0, 2))
    reord_lanes = jnp.transpose(reordered, (1, 0, 2))
    kernel = impulse.reshape(local_bundles, lag_count, bundle_width, bundle_width)
    zero_pad = jnp.zeros((local_bundles, tile_rows, bundle_width, bundle_width), jnp.bfloat16)
    kernel_pad = jnp.concatenate([zero_pad, kernel, zero_pad], axis=1)
    toeplitz = jnp.stack(
        [
            kernel_pad[:, tile_rows - shift_row : tile_rows - shift_row + lag_count + tile_rows]
            for shift_row in range(tile_rows)
        ],
        axis=3,
    )
    toeplitz = toeplitz.reshape(
        local_bundles, (lag_count + tile_rows) * bundle_width, tile_rows * bundle_width
    )
    block_rows = min(512, seg_rows)
    block_count = seg_rows // block_rows
    tile_count = block_rows // tile_rows
    behind = passed_along(masked[seg_rows - all_lags :], "tm", 1)
    history = jnp.concatenate([behind, masked], axis=0)
    hist_lanes = jnp.transpose(history, (1, 0, 2))

    def advance(grad_acc, block_index):
        row_start = block_index * block_rows
        wide = tiles_of(ext_lanes, row_start + lag_first, block_rows, lag_count)
        dx_block = jnp.einsum("bkx,bxy->bky", wide, toeplitz, preferred_element_type=jnp.float32)
        row_block = lax.dynamic_slice_in_dim(reord_lanes, row_start, block_rows, 1).reshape(
            local_bundles, tile_count, tile_rows * bundle_width
        )
        earlier = tiles_of(
            hist_lanes, row_start + all_lags - lag_first - lag_count, block_rows, lag_count
        )
        grad_acc = grad_acc + jnp.einsum(
            "bkx,bky->bxy", row_block, earlier, preferred_element_type=jnp.float32
        )
        return (grad_acc, dx_block.reshape(local_bundles, block_rows, bundle_width))

    acc_shape = (local_bundles, tile_rows * bundle_width, (lag_count + tile_rows) * bundle_width)
    grad_total, dx_blocks = lax.scan(
        advance, jnp.zeros(acc_shape, jnp.float32), jnp.arange(block_count, dtype=jnp.int32)
    )
    partial_dx = jnp.transpose(dx_blocks, (0, 2, 1, 3)).reshape(
        seg_rows, local_bundles * bundle_width
    )
    folded = grad_total.reshape(
        local_bundles, tile_rows, bundle_width, lag_count + tile_rows, bundle_width
    )
    lag_sum = folded[:, 0, :, 1 : lag_count + 1, :]
    for shift_row in range(1, tile_rows):
        lag_sum = lag_sum + folded[:, shift_row, :, shift_row + 1 : shift_row + lag_count + 1, :]
    grad_blocks = jnp.transpose(jnp.flip(lag_sum, axis=2), (0, 2, 1, 3))
    summed_dx = lax.psum_scatter(partial_dx, "sub", scatter_dimension=0, tiled=True)
    share_rows = summed_dx.shape[0]
    own_steps = (
        seg_start + lax.axis_index("sub") * share_rows + jnp.arange(share_rows, dtype=jnp.int32)
    )
    voltage_grad = jnp.where((own_steps >= fault_step[0])[:, None], summed_dx, 0.0).astype(
        jnp.bfloat16
    )
    grad_flat = grad_blocks.reshape(local_bundles, lag_count, bundle_width * bundle_width)
    grad_sum = lax.psum(grad_flat, "tm")
    share_cols = grad_flat.shape[2] // lax.axis_size("tm")
    own_grad = lax.dynamic_slice_in_dim(grad_sum, lax.axis_index("tm") * share_cols, share_cols, 2)
    own_squares = jnp.sum(own_grad * own_grad)
    total_squares = lax.psum(own_squares, ("tm", "bundle", "sub"))
    norm_limit = norm_ratio * math.sqrt(NB * L * CB * CB)
    factor = norm_limit / jnp.sqrt(total_squares + 1e-06)
    return (voltage_grad, own_grad * factor)


def solution(mesh):
    placed = (
        P(("case", "tm"), "bundle"),
        P(("case", "tm"), "bundle"),
        P("bundle", "sub", None),
        P("bundle", None),
        P("case"),
    )
    return jax.shard_map(
        local,
        mesh=mesh,
        in_specs=placed,
        out_specs=(P(("case", "tm", "sub"), "bundle"), P(("case", "bundle"), "sub", "tm")),
        check_vma=False,
    )
```

profile of v0, /device:TPU:0, one launch (start us, length us, event | category | flops | bytes accessed | tf_op | source)
XLA Modules:
  0.0 749.6 jit_solution(2607385197991196513)
XLA Ops:
  8.1 1.6 copy.41
  9.6 2.1 convolution_convert_fusion
  15.3 5.6 collective-permute-start
  20.9 4.8 copy.43
  25.6 6.1 bitcast_dynamic-update-slice_fusion
  32.8 4.1 pad_maximum_fusion
  36.9 3.3 fusion.7
  40.2 3.2 fusion.6
  43.4 3.2 fusion.5
  46.6 3.2 fusion.4
  49.9 3.2 fusion.3
  53.1 3.3 fusion.2
  56.4 3.4 fusion.1
  59.8 47.4 %copy.50 = bf16[4,72,64,8,64]{4,3,2,1,0:T(8,128)(2,1)} copy(bf16[4,72,64,8,64]{1,4,3,2,0:T(8,128)(2,1)} %fusion.1) | data formatting | bytes 37748736 | tf_op jit(solution)/shard_map/stack | solution.py:59
  107.2 49.1 %reshape.92 = bf16[4,4608,512]{2,1,0:T(8,128)(2,1)} reshape(bf16[4,72,64,8,64]{4,3,2,1,0:T(8,128)(2,1)} %copy.50) | data formatting | bytes 37748736 | tf_op jit(solution)/shard_map/reshape | solution.py:66
  156.3 2.3 maximum_bitcast_fusion.1
  159.7 269.9 %while.17 = (s32[]{:T(128)}, f32[4,512,4608]{2,1,0:T(8,128)}, f32[4,4,512,64]{3,2,1,0:T(8,128)}, s32[4]{0:T(128)S(1)}, bf16[4,2048,64]{1,2,0:T(8,128)(2,1)}, /*i...) while((s32[]{:T(128)}, f32[4,512,4608]{2,1,0:T(8,128)}, ...), condition=%wide.region_1.2_spmd.clone, body=%wide.region_0.1_spmd.clone.sunk | while | flops 2434793472 | bytes 131072384 | solution.py:92
  163.2 1.5 constant_dynamic-slice_fusion.6
  173.4 6.1 reshape.109
  179.5 8.1 %fusion.24 = f32[4,64,512]{2,1,0:T(8,128)S(1)} fusion(bf16[4,64,4608]{2,1,0:T(8,128)(2,1)S(1)} %reshape.109, bf16[4,4608,512]{2,1,0:T(8,128)(2,1)} %get-tuple-element.366), kind=kOutput, calls=%fused_computation.58.clone.1 | convolution fusion | flops 1207959552 | bytes 21757952 | tf_op jit(solution)/shard_map/while/body/eval_jaxpr/bkx,bxy->bky/dot_general | solution.py:79
  196.9 6.1 reshape.108
  203.1 14.0 %select_add_fusion.2 = f32[4,512,4608]{2,1,0:T(8,128)} fusion(f32[4,512,4608]{2,1,0:T(8,128)} %get-tuple-element.342, pred[]{:T(512)S(6)} %compare.4, bf16[4,64,512]{2,1,0:T(8,128)(2,1)S(1)} %copy-done.1, bf16[4,64,4608]{2,1,0:T(8,128)(2,1)S(1)} %reshape.108), kind=kOutput, calls=%fused_computation.clone.1 | convolution fusion | flops 1226833920 | bytes 78118912 | tf_op jit(solution)/shard_map/while/body/eval_jaxpr/bkx,bky->bxy/dot_general | solution.py:86
  220.6 1.5 constant_dynamic-slice_fusion.6
  230.8 6.1 reshape.109
  236.9 8.1 %fusion.24 = f32[4,64,512]{2,1,0:T(8,128)S(1)} fusion(bf16[4,64,4608]{2,1,0:T(8,128)(2,1)S(1)} %reshape.109, bf16[4,4608,512]{2,1,0:T(8,128)(2,1)} %get-tuple-element.366), kind=kOutput, calls=%fused_computation.58.clone.1 | convolution fusion | flops 1207959552 | bytes 21757952 | tf_op jit(solution)/shard_map/while/body/eval_jaxpr/bkx,bxy->bky/dot_general | solution.py:79
  254.4 6.1 reshape.108
  260.5 27.4 %select_add_fusion.2 = f32[4,512,4608]{2,1,0:T(8,128)} fusion(f32[4,512,4608]{2,1,0:T(8,128)} %get-tuple-element.342, pred[]{:T(512)S(6)} %compare.4, bf16[4,64,512]{2,1,0:T(8,128)(2,1)S(1)} %copy-done.1, bf16[4,64,4608]{2,1,0:T(8,128)(2,1)S(1)} %reshape.108), kind=kOutput, calls=%fused_computation.clone.1 | convolution fusion | flops 1226833920 | bytes 78118912 | tf_op jit(solution)/shard_map/while/body/eval_jaxpr/bkx,bky->bxy/dot_general | solution.py:86
  291.5 1.5 constant_dynamic-slice_fusion.6
  301.6 6.1 reshape.109
  307.8 8.1 %fusion.24 = f32[4,64,512]{2,1,0:T(8,128)S(1)} fusion(bf16[4,64,4608]{2,1,0:T(8,128)(2,1)S(1)} %reshape.109, bf16[4,4608,512]{2,1,0:T(8,128)(2,1)} %get-tuple-element.366), kind=kOutput, calls=%fused_computation.58.clone.1 | convolution fusion | flops 1207959552 | bytes 21757952 | tf_op jit(solution)/shard_map/while/body/eval_jaxpr/bkx,bxy->bky/dot_general | solution.py:79
  325.2 6.1 reshape.108
  331.4 27.4 %select_add_fusion.2 = f32[4,512,4608]{2,1,0:T(8,128)} fusion(f32[4,512,4608]{2,1,0:T(8,128)} %get-tuple-element.342, pred[]{:T(512)S(6)} %compare.4, bf16[4,64,512]{2,1,0:T(8,128)(2,1)S(1)} %copy-done.1, bf16[4,64,4608]{2,1,0:T(8,128)(2,1)S(1)} %reshape.108), kind=kOutput, calls=%fused_computation.clone.1 | convolution fusion | flops 1226833920 | bytes 78118912 | tf_op jit(solution)/shard_map/while/body/eval_jaxpr/bkx,bky->bxy/dot_general | solution.py:86
  362.3 1.4 constant_dynamic-slice_fusion.6
  372.4 6.1 reshape.109
  378.6 8.1 %fusion.24 = f32[4,64,512]{2,1,0:T(8,128)S(1)} fusion(bf16[4,64,4608]{2,1,0:T(8,128)(2,1)S(1)} %reshape.109, bf16[4,4608,512]{2,1,0:T(8,128)(2,1)} %get-tuple-element.366), kind=kOutput, calls=%fused_computation.58.clone.1 | convolution fusion | flops 1207959552 | bytes 21757952 | tf_op jit(solution)/shard_map/while/body/eval_jaxpr/bkx,bxy->bky/dot_general | solution.py:79
  396.0 6.1 reshape.108
  402.2 27.4 %select_add_fusion.2 = f32[4,512,4608]{2,1,0:T(8,128)} fusion(f32[4,512,4608]{2,1,0:T(8,128)} %get-tuple-element.342, pred[]{:T(512)S(6)} %compare.4, bf16[4,64,512]{2,1,0:T(8,128)(2,1)S(1)} %copy-done.1, bf16[4,64,4608]{2,1,0:T(8,128)(2,1)S(1)} %reshape.108), kind=kOutput, calls=%fused_computation.clone.1 | convolution fusion | flops 1226833920 | bytes 78118912 | tf_op jit(solution)/shard_map/while/body/eval_jaxpr/bkx,bky->bxy/dot_general | solution.py:86
  429.6 3.7 copy.54
  433.3 2.2 copy.60
  435.6 54.3 %reshape.94 = f32[4,8,64,72,64]{4,3,2,1,0:T(8,128)} reshape(f32[4,512,4608]{2,1,0:T(8,128)} %get-tuple-element.183) | data formatting | bytes 75497472 | tf_op jit(solution)/shard_map/reshape | solution.py:98
  489.9 27.4 %fusion = f32[4,64,64,64]{3,2,1,0:T(8,128)} fusion(f32[4,8,64,72,64]{4,3,2,1,0:T(8,128)} %reshape.94), kind=kLoop, calls=%fused_computation.24 | loop fusion | flops 7340032 | bytes 37748736 | tf_op jit(solution)/shard_map/add | solution.py:103
  517.3 11.9 %rev.4 = f32[4,64,64,64]{3,2,1,0:T(8,128)} reverse(f32[4,64,64,64]{3,2,1,0:T(8,128)} %fusion), dimensions={2} | reverse | bytes 8388608 | tf_op jit(solution)/shard_map/jit(_flip)/rev | solution.py:104
  529.1 11.5 %copy.55 = f32[4,64,64,64]{3,2,1,0:T(8,128)} copy(f32[4,64,64,64]{3,1,2,0:T(8,128)} %bitcast.113) | data formatting | bytes 8388608 | tf_op jit(solution)/shard_map/transpose | solution.py:104
  540.6 7.9 %reshape.95 = f32[4,64,4096]{2,1,0:T(8,128)} reshape(f32[4,64,64,64]{3,2,1,0:T(8,128)} %copy.55) | data formatting | bytes 8388608 | tf_op jit(solution)/shard_map/reshape | solution.py:113
  549.9 154.3 %all-reduce.3.cloned.1.call-done = f32[4,64,4096]{2,1,0:T(8,128)} async-done(((f32[4,64,4096]{2,1,0:T(8,128)}), f32[4,64,4096]{2,1,0:T(8,128)}) %all-reduce.3.cloned.1.call-update) | async-done | bytes 4194320 | tf_op jit(solution)/shard_map/psum | solution.py:114
  704.2 2.1 multiply_reduce_fusion
  707.3 31.9 %psum.15 = f32[]{:T(128)} all-reduce(f32[]{:T(128)} %multiply_reduce_fusion), channel_id=1, replica_groups=mesh['case'=2,'tm'=4,'bundle'=2,'sub'=2] {'tm','bundle','sub'}, use_global_device_ids=true, to_apply=%region_5.6 | all-reduce | flops 1 | bytes 8 | tf_op jit(solution)/shard_map/psum | solution.py:118
  739.9 2.3 dynamic-slice_multiply_fusion
  (137 shorter events, 90.5 us)
Async XLA Ops:
  8.0 6.5 copy-start.2
  8.0 540.5 %reduce-scatter.2.cloned.1.call-start = ((), (), s32[]{:S(2)}) async-start(), calls=%async_computation.1 | async-start | bytes 3145728 | tf_op jit(solution)/shard_map/reduce_scatter | solution.py:105
  12.5 143.7 %collective-permute-start.1 = (bf16[128,4,64]{0,2,1:T(8,128)(2,1)S(1)}, bf16[128,4,64]{0,2,1:T(8,128)(2,1)S(1)}, u32[]{:S(2)}, u32[]{:S(2)}) collective-permute-start(bf16[128,4,64]{0,2,1:T(8,128)(2,1)S(1)} %slice.269), channel_id=1, source_target_pairs={{4,0},{8,4},{12,8},{5,1},{9,5},{13,9},{6,2},{10,6},{14,10},{7,3},{... | collective-permute-start | bytes 196616 | tf_op jit(solution)/shard_map/ppermute | solution.py:17
  15.3 143.3 %collective-permute-start = (bf16[128,4,64]{0,2,1:T(8,128)(2,1)S(1)}, bf16[128,4,64]{0,2,1:T(8,128)(2,1)S(1)}, u32[]{:S(2)}, u32[]{:S(2)}) collective-permute-start(bf16[128,4,64]{0,2,1:T(8,128)(2,1)S(1)} %slice.268), channel_id=1, source_target_pairs={{0,4},{4,8},{8,12},{1,5},{5,9},{9,13},{2,6},{6,10},{10,14},{3,7},{... | collective-permute-start | bytes 196616 | tf_op jit(solution)/shard_map/ppermute | solution.py:17
  25.6 7.2 copy-start
  195.2 7.9 %copy-start.1 = (bf16[4,64,512]{2,1,0:T(8,128)(2,1)S(1)}, bf16[4,64,512]{2,1,0:T(8,128)(2,1)}, u32[]{:S(2)}) copy-start(bf16[4,64,512]{2,1,0:T(8,128)(2,1)} %reshape.107) | copy-start | bytes 786436 | tf_op jit(solution)/shard_map/while
  252.6 7.9 %copy-start.1 = (bf16[4,64,512]{2,1,0:T(8,128)(2,1)S(1)}, bf16[4,64,512]{2,1,0:T(8,128)(2,1)}, u32[]{:S(2)}) copy-start(bf16[4,64,512]{2,1,0:T(8,128)(2,1)} %reshape.107) | copy-start | bytes 786436 | tf_op jit(solution)/shard_map/while
  323.4 7.9 %copy-start.1 = (bf16[4,64,512]{2,1,0:T(8,128)(2,1)S(1)}, bf16[4,64,512]{2,1,0:T(8,128)(2,1)}, u32[]{:S(2)}) copy-start(bf16[4,64,512]{2,1,0:T(8,128)(2,1)} %reshape.107) | copy-start | bytes 786436 | tf_op jit(solution)/shard_map/while
  394.2 7.9 %copy-start.1 = (bf16[4,64,512]{2,1,0:T(8,128)(2,1)S(1)}, bf16[4,64,512]{2,1,0:T(8,128)(2,1)}, u32[]{:S(2)}) copy-start(bf16[4,64,512]{2,1,0:T(8,128)(2,1)} %reshape.107) | copy-start | bytes 786436 | tf_op jit(solution)/shard_map/while
  435.5 268.7 %all-reduce.3.cloned.1.call-start = ((), (), s32[]{:S(2)}) async-start(), calls=%async_computation.2 | async-start | bytes 8388608 | tf_op jit(solution)/shard_map/psum | solution.py:114
Sparse Core Ops, SparseCore 0:
  435.7 10.2 reduce-scatter.1
Sparse Core Ops, SparseCore 1:
  548.6 155.6 all-reduce.2
where the time goes:
time: 755 us; the launch traced here: 750 us
  local copies, waits for them, and re-layouts  365 us (48%)
  waiting for transfers between devices  154 us (20%)
  matrix products  131 us (17%)
  other arithmetic  40.7 us (5%)
  blocking collectives  31.9 us (4%)
  between operations  17 us (2%)
    psum x1, waiting for transfers between devices, local(): grad_sum = lax.psum(grad_flat, 'tm')  154 us
    dot_general x4, matrix products, advance(): jnp.einsum('bkx,bky->bxy', row_block, earlier, preferred_element_type=jnp...  96.3 us
    while x72, local copies, waits for them, and re-layouts  56.9 us
    reshape x1, local copies, waits for them, and re-layouts, local(): grad_total.reshape(local_bundles, tile_rows, bundle_width, lag_count + ti...  54.3 us
    another operation x2, local copies, waits for them, and re-layouts, local(): jnp.stack([kernel_pad[:, tile_rows - shift_row:tile_rows - shift_row + la...  50.8 us
    reshape x8, local copies, waits for them, and re-layouts, tiles_of(): return wide.reshape(bundles, tile_count, (lag_count + tile_rows) * width)  49.2 us
    reshape x1, local copies, waits for them, and re-layouts, local(): toeplitz.reshape(local_bundles, (lag_count + tile_rows) * bundle_width, t...  49.1 us
    unnamed x16, local copies, waits for them, and re-layouts  35.8 us
  transfers between devices with their start and end apart: 4, of which 1 were waited for; matrix products, arithmetic and copies ran while one was open for 34% of the time, Pallas kernels for 0%

commit v1 on v0

--- a/solution.py
+++ b/solution.py
@@ -111,7 +111,8 @@
         jnp.bfloat16
     )
     grad_flat = grad_blocks.reshape(local_bundles, lag_count, bundle_width * bundle_width)
-    grad_sum = lax.psum(grad_flat, "tm")
+    v_next = jax.lax.all_gather(grad_flat, axis_name="tm")
+    grad_sum = jnp.sum(v_next, axis=0)
     share_cols = grad_flat.shape[2] // lax.axis_size("tm")
     own_grad = lax.dynamic_slice_in_dim(grad_sum, lax.axis_index("tm") * share_cols, share_cols, 2)
     own_squares = jnp.sum(own_grad * own_grad)

time: 755 us -> 896 us (1.19)
  waiting for transfers between devices: 154 us -> 286 us
  other arithmetic: 40.7 us -> 50.5 us
    all_gather x0 -> x1, waiting for transfers between devices: none -> 286 us  [local(): v_next = jax.lax.all_gather(grad_flat, axis_name='tm')]
    psum x1 -> x0, waiting for transfers between devices: 154 us -> none  [local(): grad_sum = lax.psum(grad_flat, 'tm')]
    reduce_sum x0 -> x1, other arithmetic: none -> 9.83 us  [local(): grad_sum = jnp.sum(v_next, axis=0)]
  transfers between devices with their start and end apart: 4 -> 4, of which waited for: 1 -> 1; matrix products, arithmetic and copies ran while one was open for 34% -> 28% of each run, Pallas kernels for 0% -> 0%
where the time goes in v1:
time: 896 us; the launch traced here: 890 us
  local copies, waits for them, and re-layouts  365 us (41%)
  waiting for transfers between devices  286 us (32%)
  matrix products  131 us (15%)
  other arithmetic  50.5 us (6%)
  blocking collectives  31.1 us (3%)
  between operations  17 us (2%)
    all_gather x1, waiting for transfers between devices, local(): v_next = jax.lax.all_gather(grad_flat, axis_name='tm')  286 us
    dot_general x4, matrix products, advance(): jnp.einsum('bkx,bky->bxy', row_block, earlier, preferred_element_type=jnp...  96.3 us
    while x72, local copies, waits for them, and re-layouts  56.9 us
    reshape x1, local copies, waits for them, and re-layouts, local(): grad_total.reshape(local_bundles, tile_rows, bundle_width, lag_count + ti...  54.3 us
    another operation x2, local copies, waits for them, and re-layouts, local(): jnp.stack([kernel_pad[:, tile_rows - shift_row:tile_rows - shift_row + la...  50.8 us
    reshape x8, local copies, waits for them, and re-layouts, tiles_of(): return wide.reshape(bundles, tile_count, (lag_count + tile_rows) * width)  49.2 us
    reshape x1, local copies, waits for them, and re-layouts, local(): toeplitz.reshape(local_bundles, (lag_count + tile_rows) * bundle_width, t...  49.1 us
    unnamed x16, local copies, waits for them, and re-layouts  35.8 us
  transfers between devices with their start and end apart: 4, of which 1 were waited for; matrix products, arithmetic and copies ran while one was open for 28% of the time, Pallas kernels for 0%

profile of v1, /device:TPU:0, one launch (start us, length us, event | category | flops | bytes accessed | tf_op | source)
XLA Modules:
  0.0 890.5 jit_solution(18398430776943319287)
XLA Ops:
  8.1 1.6 copy.34
  9.6 2.1 convolution_convert_fusion
  15.3 5.6 collective-permute-start
  20.9 4.8 copy.36
  25.6 6.1 bitcast_dynamic-update-slice_fusion
  32.8 4.1 pad_maximum_fusion
  36.9 3.3 fusion.7
  40.2 3.2 fusion.6
  43.4 3.2 fusion.5
  46.6 3.2 fusion.4
  49.9 3.2 fusion.3
  53.1 3.3 fusion.2
  56.4 3.4 fusion.1
  59.8 47.4 %copy.43 = bf16[4,72,64,8,64]{4,3,2,1,0:T(8,128)(2,1)} copy(bf16[4,72,64,8,64]{1,4,3,2,0:T(8,128)(2,1)} %fusion.1) | data formatting | bytes 37748736 | tf_op jit(solution)/shard_map/stack | solution.py:59
  107.2 49.1 %reshape.89 = bf16[4,4608,512]{2,1,0:T(8,128)(2,1)} reshape(bf16[4,72,64,8,64]{4,3,2,1,0:T(8,128)(2,1)} %copy.43) | data formatting | bytes 37748736 | tf_op jit(solution)/shard_map/reshape | solution.py:66
  156.3 2.3 maximum_bitcast_fusion.1
  159.7 269.9 %while.17 = (s32[]{:T(128)}, f32[4,512,4608]{2,1,0:T(8,128)}, f32[4,4,512,64]{3,2,1,0:T(8,128)}, s32[4]{0:T(128)S(1)}, bf16[4,2048,64]{1,2,0:T(8,128)(2,1)}, /*i...) while((s32[]{:T(128)}, f32[4,512,4608]{2,1,0:T(8,128)}, ...), condition=%wide.region_1.2_spmd.clone, body=%wide.region_0.1_spmd.clone.sunk | while | flops 2434793472 | bytes 131072384 | solution.py:92
  163.2 1.5 constant_dynamic-slice_fusion.6
  173.4 6.1 reshape.105
  179.5 8.1 fusion.24
  196.9 6.1 reshape.104
  203.1 14.0 %select_add_fusion.2 = f32[4,512,4608]{2,1,0:T(8,128)} fusion(f32[4,512,4608]{2,1,0:T(8,128)} %get-tuple-element.342, pred[]{:T(512)S(6)} %compare.4, bf16[4,64,512]{2,1,0:T(8,128)(2,1)S(1)} %copy-done.1, bf16[4,64,4608]{2,1,0:T(8,128)(2,1)S(1)} %reshape.104), kind=kOutput, calls=%fused_computation.clone.1 | convolution fusion | flops 1226833920 | bytes 78118912 | tf_op jit(solution)/shard_map/while/body/eval_jaxpr/bkx,bky->bxy/dot_general | solution.py:86
  220.6 1.5 constant_dynamic-slice_fusion.6
  230.8 6.1 reshape.105
  236.9 8.1 fusion.24
  254.4 6.1 reshape.104
  260.5 27.4 %select_add_fusion.2 = f32[4,512,4608]{2,1,0:T(8,128)} fusion(f32[4,512,4608]{2,1,0:T(8,128)} %get-tuple-element.342, pred[]{:T(512)S(6)} %compare.4, bf16[4,64,512]{2,1,0:T(8,128)(2,1)S(1)} %copy-done.1, bf16[4,64,4608]{2,1,0:T(8,128)(2,1)S(1)} %reshape.104), kind=kOutput, calls=%fused_computation.clone.1 | convolution fusion | flops 1226833920 | bytes 78118912 | tf_op jit(solution)/shard_map/while/body/eval_jaxpr/bkx,bky->bxy/dot_general | solution.py:86
  291.5 1.5 constant_dynamic-slice_fusion.6
  301.6 6.1 reshape.105
  307.8 8.1 fusion.24
  325.2 6.1 reshape.104
  331.4 27.4 %select_add_fusion.2 = f32[4,512,4608]{2,1,0:T(8,128)} fusion(f32[4,512,4608]{2,1,0:T(8,128)} %get-tuple-element.342, pred[]{:T(512)S(6)} %compare.4, bf16[4,64,512]{2,1,0:T(8,128)(2,1)S(1)} %copy-done.1, bf16[4,64,4608]{2,1,0:T(8,128)(2,1)S(1)} %reshape.104), kind=kOutput, calls=%fused_computation.clone.1 | convolution fusion | flops 1226833920 | bytes 78118912 | tf_op jit(solution)/shard_map/while/body/eval_jaxpr/bkx,bky->bxy/dot_general | solution.py:86
  372.4 6.1 reshape.105
  378.6 8.1 fusion.24
  396.0 6.1 reshape.104
  402.2 27.4 %select_add_fusion.2 = f32[4,512,4608]{2,1,0:T(8,128)} fusion(f32[4,512,4608]{2,1,0:T(8,128)} %get-tuple-element.342, pred[]{:T(512)S(6)} %compare.4, bf16[4,64,512]{2,1,0:T(8,128)(2,1)S(1)} %copy-done.1, bf16[4,64,4608]{2,1,0:T(8,128)(2,1)S(1)} %reshape.104), kind=kOutput, calls=%fused_computation.clone.1 | convolution fusion | flops 1226833920 | bytes 78118912 | tf_op jit(solution)/shard_map/while/body/eval_jaxpr/bkx,bky->bxy/dot_general | solution.py:86
  429.6 3.7 copy.47
  433.3 2.2 copy.53
  435.6 54.3 %reshape.91 = f32[4,8,64,72,64]{4,3,2,1,0:T(8,128)} reshape(f32[4,512,4608]{2,1,0:T(8,128)} %get-tuple-element.183) | data formatting | bytes 75497472 | tf_op jit(solution)/shard_map/reshape | solution.py:98
  489.9 27.4 %fusion = f32[4,64,64,64]{3,2,1,0:T(8,128)} fusion(f32[4,8,64,72,64]{4,3,2,1,0:T(8,128)} %reshape.91), kind=kLoop, calls=%fused_computation.24 | loop fusion | flops 7340032 | bytes 37748736 | tf_op jit(solution)/shard_map/add | solution.py:103
  517.3 11.9 %rev.4 = f32[4,64,64,64]{3,2,1,0:T(8,128)} reverse(f32[4,64,64,64]{3,2,1,0:T(8,128)} %fusion), dimensions={2} | reverse | bytes 8388608 | tf_op jit(solution)/shard_map/jit(_flip)/rev | solution.py:104
  529.1 11.5 %copy.48 = f32[4,64,64,64]{3,2,1,0:T(8,128)} copy(f32[4,64,64,64]{3,1,2,0:T(8,128)} %bitcast.113) | data formatting | bytes 8388608 | tf_op jit(solution)/shard_map/transpose | solution.py:104
  540.6 7.9 all_gather_reshape.3
  549.9 286.1 %all-gather.2.cloned.1.call-done = f32[4,4,64,4096]{3,2,1,0:T(8,128)} async-done(((f32[1,4,64,4096]{3,2,1,0:T(8,128)}), f32[4,4,64,4096]{3,2,1,0:T(8,128)}) %all-gather.2.cloned.1.call-update) | async-done | bytes 16777232 | tf_op jit(solution)/shard_map/all_gather | solution.py:114
  836.0 9.8 %reduce_sum.18 = f32[4,64,4096]{2,1,0:T(8,128)} reduce(f32[4,4,64,4096]{3,2,1,0:T(8,128)} %all-gather.2.cloned.1.call-done, f32[]{:T(128)} %constant.91.clone.1), dimensions={0}, to_apply=%region_3.4 | reduce | flops 3145728 | bytes 20971524 | tf_op jit(solution)/shard_map/reduce_sum | solution.py:115
  845.9 2.1 multiply_reduce_fusion
  848.9 31.1 %psum.7 = f32[]{:T(128)} all-reduce(f32[]{:T(128)} %multiply_reduce_fusion), channel_id=1, replica_groups=mesh['case'=2,'tm'=4,'bundle'=2,'sub'=2] {'tm','bundle','sub'}, use_global_device_ids=true, to_apply=%region_5.6 | all-reduce | flops 1 | bytes 8 | tf_op jit(solution)/shard_map/psum | solution.py:119
  880.7 2.3 dynamic-slice_multiply_fusion
  (138 shorter events, 91.9 us)
Async XLA Ops:
  8.0 6.5 copy-start.2
  8.0 540.5 %reduce-scatter.2.cloned.1.call-start = ((), (), s32[]{:S(2)}) async-start(), calls=%async_computation.1 | async-start | bytes 3145728 | tf_op jit(solution)/shard_map/reduce_scatter | solution.py:105
  12.5 143.7 %collective-permute-start.1 = (bf16[128,4,64]{0,2,1:T(8,128)(2,1)S(1)}, bf16[128,4,64]{0,2,1:T(8,128)(2,1)S(1)}, u32[]{:S(2)}, u32[]{:S(2)}) collective-permute-start(bf16[128,4,64]{0,2,1:T(8,128)(2,1)S(1)} %slice.269), channel_id=1, source_target_pairs={{4,0},{8,4},{12,8},{5,1},{9,5},{13,9},{6,2},{10,6},{14,10},{7,3},{... | collective-permute-start | bytes 196616 | tf_op jit(solution)/shard_map/ppermute | solution.py:17
  15.3 143.3 %collective-permute-start = (bf16[128,4,64]{0,2,1:T(8,128)(2,1)S(1)}, bf16[128,4,64]{0,2,1:T(8,128)(2,1)S(1)}, u32[]{:S(2)}, u32[]{:S(2)}) collective-permute-start(bf16[128,4,64]{0,2,1:T(8,128)(2,1)S(1)} %slice.268), channel_id=1, source_target_pairs={{0,4},{4,8},{8,12},{1,5},{5,9},{9,13},{2,6},{6,10},{10,14},{3,7},{... | collective-permute-start | bytes 196616 | tf_op jit(solution)/shard_map/ppermute | solution.py:17
  25.6 7.2 copy-start
  195.2 7.9 copy-start.1
  252.6 7.9 copy-start.1
  323.4 7.9 copy-start.1
  394.2 7.9 copy-start.1
  435.5 400.5 %all-gather.2.cloned.1.call-start = ((), (), s32[]{:S(2)}) async-start(), calls=%async_computation.2 | async-start | bytes 20971520 | tf_op jit(solution)/shard_map/all_gather | solution.py:114
Sparse Core Ops, SparseCore 0:
  435.7 10.2 reduce-scatter.1
Sparse Core Ops, SparseCore 1:
  548.6 287.4 all-gather.1
